TPU v7x, 128 devices: a whole 4x4x4 slice. The times are simulated.
128 devices in a mesh: seq: 32 (over x, z, core), tp: 4 (over y).
Axes of the slice: x: 4, y: 4, z: 4, core: 2. Of those that a mesh axis runs over, the one named last changes fastest.
Arguments:
- tokens: bfloat16 [8192, 2048], P('seq'), may hold values from -6 to 6
- norm_gain: float32 [2048], replicated, may hold values from 0.1 to 1.9
- qkv_weight: bfloat16 [2048, 4096], P(None, 'tp'), may hold values from -0.125 to 0.125
- conv_weight: float32 [4, 4096], P(None, 'tp'), may hold values from -3 to 3
- gate_down: bfloat16 [2048, 16], replicated, may hold values from -0.125 to 0.125
- gate_up: bfloat16 [16, 1024], P(None, 'tp'), may hold values from -6 to 6
- gate_bias: float32 [1024], P('tp'), may hold values from 0.3 to 8.5
- out_gate_weight: bfloat16 [2048, 2048], P(None, 'tp'), may hold values from -0.125 to 0.125
- head_gain: float32 [512], replicated, may hold values from 0.1 to 1.9
- out_weight: bfloat16 [2048, 2048], P('tp'), may hold values from -0.125 to 0.125
- final_gain: float32 [2048], replicated, may hold values from 0.1 to 1.9
- embedding: bfloat16 [32000, 2048], P(('seq', 'tp')), may hold values from -0.5 to 0.5
- lengths: int32 [8], replicated, may hold values from 1 to 4096, as said below
- packed_order: int32 [8], replicated, may hold values from 0 to 7, each once
Outputs:
- hidden: bfloat16 [8192, 2048], P('seq', 'tp')
- last_states: float32 [8, 4, 256, 512], P(None, 'tp')
- conv_edges: float32 [8, 3, 4096], P(None, None, 'tp')
- last_norms: float32 [8], replicated
- max_logits: float32 [8, 128], P(None, ('seq', 'tp'))
Inputs may be any that keep to these rules, and one draw needn't show every extreme that they name: Request r of the initial order has lengths[r] tokens; the lengths sum to 8192, the largest is 4096 and the smallest is 1 or 2. packed_order names every request once; the packed positions hold the tokens of request packed_order[0], then those of packed_order[1], and so on.
All inputs are finite; a program needn't handle non-finite values.
Results may differ from a plain program's by a relative error of at most 0.015.
Values may be sent and summed in bfloat16 or wider, within the bound.
No kernel may reach another device: no remote copies, remote signals or barrier semaphores. Data moves between devices by JAX's collectives and lax.ppermute only.
A program may use at most 128 MiB of HBM per device.

v0:
```python
from functools import partial
import jax
import jax.numpy as jnp
from jax import lax
from jax.sharding import PartitionSpec as P

DK = 256
DV = 512
KCONV = 4
BLOCK = 64
HIGHEST_PRECISION = lax.Precision.HIGHEST


def prefix(array, axis, combine, identity):
    peers, place = (lax.axis_size(axis), lax.axis_index(axis))
    everything = jax.tree.map(
        lambda part, kind: lax.all_gather(part.astype(kind), axis),
        array,
        (jnp.bfloat16, jnp.bfloat16),
    )
    start = jax.tree.map(
        lambda part, zero: jnp.broadcast_to(jnp.asarray(zero, part.dtype), part.shape),
        array,
        identity,
    )

    def hop(k, before):
        reached = k < place
        new = combine(
            before, jax.tree.map(lambda part, own: part[k].astype(own.dtype), everything, array)
        )
        return jax.tree.map(lambda a, b: jnp.where(reached, a, b), new, before)

    return lax.fori_loop(0, peers, hop, start)


def passed_along(array, axis, by):
    peers = lax.axis_size(axis)
    pairs = [(i, i + by) for i in range(peers) if 0 <= i + by < peers]
    return lax.ppermute(array, axis, pairs)


def segments(lengths, packed_order, positions):
    request_count = lengths.shape[0]
    select = (packed_order[:, None] == jnp.arange(request_count, dtype=jnp.int32)[None, :]).astype(
        jnp.int32
    )
    packed_len = jnp.sum(select * lengths[None, :], axis=1)
    end_points = jnp.cumsum(packed_len)
    starts = end_points - packed_len
    segment = jnp.sum((positions[:, None] >= starts[None, :]).astype(jnp.int32), axis=1) - 1
    last_index = jnp.sum(select * (end_points - 1)[:, None], axis=0)
    return (segment, last_index)


def causal_conv(padded, padded_segment, conv_weight, row_count):
    running = jnp.zeros((row_count, padded.shape[1]), jnp.float32)
    current = padded_segment[KCONV - 1 :]
    for offset in range(KCONV):
        window = padded[offset : offset + row_count]
        same_segment = (padded_segment[offset : offset + row_count] == current)[:, None]
        running = running + jnp.where(same_segment, window, 0.0) * conv_weight[offset]
    return running


def activate(convolved, head_count):
    shaped = convolved.reshape(convolved.shape[0], head_count, 2 * DK + DV)
    channel = jnp.arange(2 * DK + DV)
    return jnp.where(channel < 2 * DK, jax.nn.silu(shaped), shaped).astype(jnp.bfloat16)


def advance(carry_state, key_floats, values, cumulative, segment, segment_before):
    total_decay = cumulative[-1]
    same_tail = (segment == segment[-1])[:, None, None]
    scaled = jnp.where(same_tail, key_floats * jnp.exp(total_decay[None] - cumulative), 0.0).astype(
        jnp.bfloat16
    )
    added = jnp.einsum("jhc,jhv->hcv", scaled, values, preferred_element_type=jnp.float32)
    through = segment[-1] == segment_before
    return jnp.where(through, jnp.exp(total_decay)[:, :, None] * carry_state, 0.0) + added


def state_at_ends(
    end_states, carry_state, key_floats, values, cumulative, segment, segment_before, offset
):
    length = segment.shape[0]
    inside_block = (offset >= 0) & (offset < length)

    def add_ends(previous):
        end_row = jnp.clip(offset, 0, length - 1)
        end_decay = cumulative[end_row]
        end_segment = segment[end_row]
        indices = jnp.arange(length)
        allowed = (
            (indices[None, :] <= end_row[:, None]) & (segment[None, :] == end_segment[:, None])
        )[:, :, None, None]
        spread = jnp.where(allowed, end_decay[:, None] - cumulative[None], 0.0)
        weighted = jnp.where(allowed, key_floats[None] * jnp.exp(spread), 0.0).astype(jnp.bfloat16)
        within = jnp.einsum("rjhc,jhv->rhcv", weighted, values, preferred_element_type=jnp.float32)
        carried = (end_segment == segment_before)[:, None, None, None]
        reached = jnp.where(carried, jnp.exp(end_decay)[:, :, :, None] * carry_state[None], 0.0)
        return jnp.where(inside_block[:, None, None, None], within + reached, previous)

    def keep(previous):
        return previous

    return lax.cond(jnp.any(inside_block), add_ends, keep, end_states)


def block_step(last_index, carry, inputs):
    carry_state, end_states = carry
    queries, key_rows, values, decays, segment, segment_before, block_first = inputs
    cumulative = jnp.cumsum(decays, axis=0)
    length = segment.shape[0]
    indices = jnp.arange(length)
    causal = (indices[None, :] <= indices[:, None]) & (segment[None, :] == segment[:, None])
    allowed = causal[:, :, None, None]
    spread = jnp.where(allowed, cumulative[:, None] - cumulative[None, :], 0.0)
    weights = jnp.where(allowed, jnp.exp(spread), 0.0)
    query_rows = queries.astype(jnp.float32)
    key_floats = key_rows.astype(jnp.float32)
    scores = jnp.sum(query_rows[:, None] * key_floats[None, :] * weights, axis=-1).astype(
        jnp.bfloat16
    )
    inside = jnp.einsum("ijh,jhv->ihv", scores, values, preferred_element_type=jnp.float32)
    carried = (segment == segment_before)[:, None, None]
    outside = jnp.einsum(
        "ihc,hcv->ihv", query_rows * jnp.exp(cumulative), carry_state, precision=HIGHEST_PRECISION
    )
    output = inside + jnp.where(carried, outside, 0.0)
    new_state = advance(carry_state, key_floats, values, cumulative, segment, segment_before)
    end_states = state_at_ends(
        end_states,
        carry_state,
        key_floats,
        values,
        cumulative,
        segment,
        segment_before,
        last_index - block_first,
    )
    return ((new_state, end_states), output)


def state_only(carry_state, inputs):
    block_queries, block_keys, block_values, block_decays, block_segment, before, block_start = (
        inputs
    )
    cumulative = jnp.cumsum(block_decays, axis=0)
    return (
        advance(
            carry_state,
            block_keys.astype(jnp.float32),
            block_values,
            cumulative,
            block_segment,
            before,
        ),
        None,
    )


def head_output(attended, gate_out, head_gain):
    row_count, head_count, value_width = attended.shape
    mean_square = jnp.mean(attended * attended, axis=2, keepdims=True)
    gate_values = jax.nn.silu(
        gate_out.astype(jnp.float32).reshape(row_count, head_count, value_width)
    )
    gated = attended * lax.rsqrt(mean_square + 1e-05) * head_gain * gate_values
    return gated.reshape(row_count, head_count * value_width).astype(jnp.bfloat16)


def carry_in(decay_factor, local_state):

    def combine(earlier, later):
        return (earlier[0] * later[0], later[0][:, :, None] * earlier[1] + later[1])

    identity = (jnp.ones_like(decay_factor), jnp.zeros_like(local_state))
    result = prefix((decay_factor, local_state), "seq", combine, identity)
    return result[1]


def shards(
    tokens,
    norm_gain,
    qkv_weight,
    conv_weight,
    gate_down,
    gate_up,
    gate_bias,
    out_gate_weight,
    head_gain,
    out_weight,
    final_gain,
    embedding,
    lengths,
    packed_order,
):
    row_count = tokens.shape[0]
    head_count = out_weight.shape[0] // DV
    column_count = tokens.shape[1] // lax.axis_size("tp")
    start_row = lax.axis_index("seq") * row_count
    positions = start_row + jnp.arange(-(KCONV - 1), row_count, dtype=jnp.int32)
    segment_all, last_index = segments(lengths, packed_order, positions)
    segment = segment_all[KCONV - 1 :]
    segment_prior = segment_all[KCONV - 2]
    first_index = last_index - lengths + 1
    residual = tokens.astype(jnp.float32)
    normed = (
        residual
        * lax.rsqrt(jnp.mean(residual * residual, axis=1, keepdims=True) + 1e-06)
        * norm_gain
    ).astype(jnp.bfloat16)
    projected = jnp.dot(normed, qkv_weight, preferred_element_type=jnp.float32).astype(jnp.bfloat16)
    rim_rows = passed_along(projected[row_count - (KCONV - 1) :], "seq", 1)
    padded = jnp.concatenate([rim_rows, projected], axis=0)
    convolved = causal_conv(padded.astype(jnp.float32), segment_all, conv_weight, row_count)
    activated = activate(convolved, head_count)
    queries = activated[:, :, :DK]
    key_rows = activated[:, :, DK : 2 * DK]
    values = activated[:, :, 2 * DK :]
    lowrank = jnp.dot(normed, gate_down, preferred_element_type=jnp.float32)
    gate_logits = (
        jnp.dot(lowrank, gate_up.astype(jnp.float32), precision=HIGHEST_PRECISION) + gate_bias
    )
    decays = (jax.nn.log_sigmoid(gate_logits) / 16.0).reshape(row_count, head_count, DK)
    gate_out = jnp.dot(normed, out_gate_weight, preferred_element_type=jnp.float32).astype(
        jnp.bfloat16
    )
    block_count = row_count // BLOCK

    def split_blocks(array):
        return array.reshape((block_count, BLOCK) + array.shape[1:])

    segment_before = segment_all[KCONV - 2 : KCONV - 2 + row_count : BLOCK]
    block_first = start_row + jnp.arange(block_count, dtype=jnp.int32) * BLOCK
    block_inputs = (
        split_blocks(queries),
        split_blocks(key_rows),
        split_blocks(values),
        split_blocks(decays),
        split_blocks(segment),
        segment_before,
        block_first,
    )
    through_shard = segment[-1] == segment_prior
    empty_state = jnp.zeros((head_count, DK, DV), jnp.float32)
    empty_ends = jnp.zeros((lengths.shape[0], head_count, DK, DV), jnp.float32)
    stepper = partial(block_step, last_index)
    local_state, unused_steps = lax.scan(state_only, empty_state, block_inputs)
    decay_factor = jnp.where(through_shard, jnp.exp(jnp.sum(decays, axis=0)), 0.0)
    incoming = carry_in(decay_factor, local_state)
    (unused_state, end_states), attended = lax.scan(stepper, (incoming, empty_ends), block_inputs)
    attended = attended.reshape(row_count, head_count, DV)
    gated = head_output(attended, gate_out, head_gain)
    projected_out = jnp.dot(gated, out_weight, preferred_element_type=jnp.float32)
    summed = lax.psum_scatter(
        projected_out.astype(jnp.bfloat16), "tp", scatter_dimension=1, tiled=True
    ).astype(jnp.float32)
    column_start = lax.axis_index("tp") * column_count
    own_columns = lax.dynamic_slice_in_dim(residual, column_start, column_count, 1)
    hidden = (own_columns + summed).astype(jnp.bfloat16)
    owned_here = (last_index >= start_row) & (last_index < start_row + row_count)
    local_last = jnp.clip(last_index - start_row, 0, row_count - 1)
    last_rows = jnp.where(owned_here[:, None], hidden[local_last].astype(jnp.float32), 0.0)
    edge_list = []
    for offset in range(KCONV - 1):
        located = last_index - (KCONV - 2) + offset
        inside = owned_here & (located >= first_index)
        picked = padded[jnp.clip(located - start_row + KCONV - 1, 0, row_count + KCONV - 2)].astype(
            jnp.float32
        )
        edge_list.append(jnp.where(inside[:, None], picked, 0.0))
    conv_edges = jnp.stack(edge_list, axis=1)
    row_sums, conv_edges, last_states = (
        lax.psum(last_rows.astype(jnp.bfloat16), "seq").astype(jnp.float32),
        lax.psum(conv_edges.astype(jnp.bfloat16), "seq").astype(jnp.float32),
        lax.psum(end_states.astype(jnp.bfloat16), "seq").astype(jnp.float32),
    )
    full_rows = lax.all_gather(row_sums, "tp", axis=1, tiled=True)
    mean_square = jnp.mean(full_rows * full_rows, axis=1)
    last_norms = jnp.sqrt(mean_square)
    final_rows = (full_rows * lax.rsqrt(mean_square[:, None] + 1e-06) * final_gain).astype(
        jnp.bfloat16
    )
    logits = jnp.dot(final_rows, embedding.T, preferred_element_type=jnp.float32)
    max_logits = jnp.max(logits, axis=1, keepdims=True)
    return (hidden, last_states, conv_edges, last_norms, max_logits)


def solution(mesh):
    in_specs = (
        P("seq", None),
        P(),
        P(None, "tp"),
        P(None, "tp"),
        P(),
        P(None, "tp"),
        P("tp"),
        P(None, "tp"),
        P(),
        P("tp", None),
        P(),
        P(("seq", "tp"), None),
        P(),
        P(),
    )
    out_specs = (
        P("seq", "tp"),
        P(None, "tp", None, None),
        P(None, None, "tp"),
        P(),
        P(None, ("seq", "tp")),
    )
    return jax.shard_map(shards, mesh=mesh, in_specs=in_specs, out_specs=out_specs, check_vma=False)
```

profile of v0, /device:TPU:0, one launch (start us, length us, event | category | flops | bytes accessed | tf_op | source)
XLA Modules:
  0.0 477.1 jit_solution(16728195551736005816)
XLA Ops:
  7.2 1.6 multiply_reduce_fusion.1
  9.0 3.9 convolution_convert_fusion.1
  14.8 1.7 fusion.70
  21.1 21.8 %while.43 = (s32[]{:T(128)}, f32[1,256,512]{2,1,0:T(8,128)S(1)}, s32[4,64]{1,0:T(4,128)S(1)}, s32[4]{0:T(128)S(1)}, f32[4,64,1,256]{3,2,1,0:T(1,128)}, /*index=5...) while((s32[]{:T(128)}, f32[1,256,512]{2,1,0:T(8,128)S(1)}, ...), condition=%wide.region_7.8_spmd.clone, body=%wide.region_5.7_spmd.clone.sunk | while | flops 18415684 | bytes 1417237 | solution.py:250
  45.5 26.3 %all-gather.2 = bf16[32,1,256]{2,1,0:T(2,128)(2,1)S(1)} all-gather(bf16[1,1,256]{2,1,0:T(2,128)(2,1)S(1)} %reshape.975), channel_id=2, replica_groups=mesh['seq'=32,'tp'=4] {'seq'}, dimensions={0}, use_global_device_ids=true | all-gather | bytes 16896 | tf_op jit(solution)/shard_map/all_gather | solution.py:17
  71.9 29.0 %all-gather.5.cloned.1.call-done = bf16[32,256,512]{2,1,0:T(8,128)(2,1)} async-done(((bf16[1,256,512]{2,1,0:T(8,128)(2,1)}), bf16[32,256,512]{2,1,0:T(8,128)(2,1)}) %all-gather.5.cloned.1.call-update) | async-done | bytes 8388624 | tf_op jit(solution)/shard_map/all_gather | solution.py:17
  101.0 36.2 %while.44 = (s32[]{:T(128)}, f32[1,256,512]{2,1,0:T(8,128)S(1)}, s32[]{:T(128)}, bf16[32,1,256]{2,1,0:T(2,128)(2,1)S(1)}, bf16[32,1,256,512]{3,2,1,0:T(8,128)(2,1)}, /*index=5*/s32[]{:T(128)}, s32[]{:T(128)}) while((s32[]{:T(128)}, f32[1,256,512]{2,1,0:T(8,128)S(1)}, s32[]{:T(128)}, bf16[32,1,256]{2,1,0:T(2,128)(2,1)S(1)}, ...), condition=%wide.region_9.10_spmd.clone, body=%wide.region_8.9_spmd.clone.sunk | while | flops 655620 | bytes 1313385 | solution.py:34
  137.1 1.5 broadcast_in_dim.240
  138.6 54.6 %while.42 = (s32[]{:T(128)}, f32[1,256,512]{2,1,0:T(8,128)S(1)}, bf16[8,1,256,512]{3,2,0,1:T(8,128)(2,1)}, f32[4,64,1,512]{3,1,2,0:T(8,128)}, s32[4,64]{1,0:T(4,...) while((s32[]{:T(128)}, f32[1,256,512]{2,1,0:T(8,128)S(1)}, ...), condition=%wide.region_17.18_spmd, body=%wide.region_11.17_spmd.sunk | while | flops 268659424 | bytes 8804605 | solution.py:253
  144.4 5.7 %conditional.2 = (bf16[8,1,256,512]{3,2,0,1:T(8,128)(2,1)}) conditional(s32[]{:T(128)} %convert_element_type.388, bf16[8,1,256,512]{3,2,0,1:T(8,128)(2,1)} %get-tuple-element.722, (pred[8]{0:T(512)(128)(4,1)S(1)}, s32[8]{0:T(128)S(1)}, s32[64]{0:T(128)S(1)}, bf16[1,64,1,256]{3,2,1,0:T(2,128)(2,1)S(1)}, f32[64,1,256]{2,1,0:T(1,128)S(1)}, ...), branch_computations={%region_14.14_spmd, %region_15.15_spmd} | conditional | flops 139086368 | bytes 5199492 | solution.py:107
  146.4 3.7 fusion
  150.3 2.0 multiply_reduce_fusion.5
  162.5 2.0 multiply_reduce_fusion.5
  174.7 2.0 multiply_reduce_fusion.5
  187.0 2.0 multiply_reduce_fusion.5
  194.5 2.8 fusion.56
  197.3 1.7 convolution_convert_fusion
  199.0 2.8 convert_element_type.287
  203.9 96.7 %all-reduce.3.cloned.1.call-done = bf16[8,1,256,512]{3,2,1,0:T(8,128)(2,1)} async-done(((bf16[8,1,256,512]{3,2,1,0:T(8,128)(2,1)}), bf16[8,1,256,512]{3,2,1,0:T(8,128)(2,1)}) %all-reduce.3.cloned.1.call-update) | async-done | bytes 2097168 | tf_op jit(solution)/shard_map/psum | solution.py:278
  300.6 4.2 convert_element_type.304
  304.8 21.7 %reduce-scatter.2.cloned.1.call-done = bf16[256,512]{1,0:T(8,128)(2,1)} async-done(((bf16[256,2048]{1,0:T(8,128)(2,1)}), bf16[256,512]{1,0:T(8,128)(2,1)}) %reduce-scatter.2.cloned.1.call-update) | async-done | bytes 262160 | tf_op jit(solution)/shard_map/reduce_scatter | solution.py:257
  328.3 126.8 %all-reduce = (bf16[8,3,1024]{2,0,1:T(8,128)(2,1)S(1)}, bf16[8,512]{1,0:T(8,128)(2,1)S(1)}) all-reduce(bf16[8,3,1024]{2,0,1:T(8,128)(2,1)S(1)} %pad_maximum_fusion.1, bf16[8,512]{1,0:T(8,128)(2,1)S(1)} %select_convert_fusion.2), channel_id=1, replica_groups=mesh['seq'=32,'tp'=4] {'seq'}, use_global_device_ids=true, to_apply=%region_21.22 | all-reduce | flops 28672 | bytes 114688 | tf_op jit(solution)/shard_map/psum | solution.py:277
  455.2 11.9 %all_gather.16 = f32[8,2048]{1,0:T(8,128)S(1)} all-gather(f32[8,512]{1,0:T(8,128)S(1)} %convert_element_type.314), channel_id=1, replica_groups=mesh['seq'=32,'tp'=4] {'tp'}, dimensions={1}, use_global_device_ids=true | all-gather | bytes 81920 | tf_op jit(solution)/shard_map/all_gather | solution.py:280
  468.3 2.2 convolution_reduce_fusion
  (283 shorter events, 100.4 us)
Async XLA Ops:
  7.2 190.1 %copy-start = (bf16[512,2048]{1,0:T(8,128)(2,1)S(1)}, bf16[512,2048]{1,0:T(8,128)(2,1)}, u32[]{:S(2)}) copy-start(bf16[512,2048]{1,0:T(8,128)(2,1)} %param.31) | copy-start | bytes 6291460
  7.2 93.8 %all-gather.5.cloned.1.call-start = ((), (), s32[]{:S(2)}) async-start(), calls=%async_computation.3 | async-start | bytes 8650752 | tf_op jit(solution)/shard_map/all_gather | solution.py:17
  8.9 5.3 %copy-start.6 = (s32[8]{0:T(128)S(1)}, s32[8]{0:T(128)}, u32[]{:S(2)}) copy-start(s32[8]{0:T(128)} %param.34) | copy-start | bytes 100
  8.9 5.3 %copy-start.12 = (s32[8]{0:T(128)S(1)}, s32[8]{0:T(128)}, u32[]{:S(2)}) copy-start(s32[8]{0:T(128)} %param.35) | copy-start | bytes 100
  8.9 5.8 %copy-start.4 = (f32[4,1024]{1,0:T(4,128)S(1)}, f32[4,1024]{1,0:T(4,128)}, u32[]{:S(2)}) copy-start(f32[4,1024]{1,0:T(4,128)} %param.25) | copy-start | bytes 49156
  8.9 5.8 %copy-start.7 = (bf16[2048,16]{0,1:T(8,128)(2,1)S(1)}, bf16[2048,16]{0,1:T(8,128)(2,1)}, u32[]{:S(2)}) copy-start(bf16[2048,16]{0,1:T(8,128)(2,1)} %param.26) | copy-start | bytes 196612
  8.9 5.8 %copy-start.9 = (f32[2048]{0:T(1024)S(1)}, f32[2048]{0:T(1024)}, u32[]{:S(2)}) copy-start(f32[2048]{0:T(1024)} %param.23) | copy-start | bytes 24580
  8.9 7.5 %copy-start.8 = (bf16[16,256]{1,0:T(8,128)(2,1)S(1)}, bf16[16,256]{1,0:T(8,128)(2,1)}, u32[]{:S(2)}) copy-start(bf16[16,256]{1,0:T(8,128)(2,1)} %param.27) | copy-start | bytes 24580
  9.0 7.5 %copy-start.11 = (f32[256]{0:T(256)S(1)}, f32[256]{0:T(256)}, u32[]{:S(2)}) copy-start(f32[256]{0:T(256)} %param.28) | copy-start | bytes 3076
  12.9 5.3 %collective-permute-start = (bf16[3,1024]{1,0:T(4,128)(2,1)S(1)}, bf16[3,1024]{1,0:T(4,128)(2,1)S(1)}, u32[]{:S(2)}, u32[]{:S(2)}) collective-permute-start(bf16[3,1024]{1,0:T(4,128)(2,1)S(1)} %slice.111), channel_id=1, source_target_pairs={{0,4},{4,8},{8,12},{12,16},{16,20},{20,24},{24,28},{28,32},{32,36}... | collective-permute-start | bytes 18440 | tf_op jit(solution)/shard_map/ppermute | solution.py:40
  43.6 257.0 %all-reduce.3.cloned.1.call-start = ((), (), s32[]{:S(2)}) async-start(), calls=%async_computation.2 | async-start | bytes 4194304 | tf_op jit(solution)/shard_map/psum | solution.py:278
  193.3 1.0 copy-start.2
  193.3 1.2 copy-start.10
  193.3 133.2 %reduce-scatter.2.cloned.1.call-start = ((), (), s32[]{:S(2)}) async-start(), calls=%async_computation.1 | async-start | bytes 1310720 | tf_op jit(solution)/shard_map/reduce_scatter | solution.py:257
  199.0 2.9 copy-start.1
  203.9 264.4 %copy-start.5 = (f32[2048]{0:T(1024)S(1)}, f32[2048]{0:T(1024)}, u32[]{:S(2)}) copy-start(f32[2048]{0:T(1024)} %param.32) | copy-start | bytes 24580
  327.7 142.9 %copy-start.3 = (bf16[256,512]{1,0:T(8,128)(2,1)}, bf16[256,512]{1,0:T(8,128)(2,1)S(1)}, u32[]{:S(2)}) copy-start(bf16[256,512]{1,0:T(8,128)(2,1)S(1)} %add_convert_fusion) | copy-start | bytes 786436
Sparse Core Ops, SparseCore 0:
  43.7 57.1 all-gather.4
  193.4 107.1 all-reduce.2
  303.0 23.4 reduce-scatter.1
where the time goes:
time: 480 us; the launch traced here: 477 us
  blocking collectives  165 us (34%)
  waiting for transfers between devices  147 us (31%)
  other arithmetic  81.7 us (17%)
  matrix products  27.2 us (6%)
  local copies, waits for them, and re-layouts  24.3 us (5%)
  between operations  15.3 us (3%)
  loops' own time  14.8 us (3%)
    psum x1, blocking collectives, shards(): lax.psum(conv_edges.astype(jnp.bfloat16), 'seq').astype(jnp.float32)  127 us
    psum x1, waiting for transfers between devices, shards(): lax.psum(end_states.astype(jnp.bfloat16), 'seq').astype(jnp.float32)  96.7 us
    select_n x32, other arithmetic, hop(): return jax.tree.map(lambda a, b: jnp.where(reached, a, b), new, before)  34.9 us
    all_gather x1, waiting for transfers between devices, prefix(): lax.all_gather(part.astype(kind), axis)  29 us
    all_gather x1, blocking collectives, prefix(): lax.all_gather(part.astype(kind), axis)  26.3 us
    reduce_scatter x1, waiting for transfers between devices, shards(): lax.psum_scatter(projected_out.astype(jnp.bfloat16), 'tp', scatter_dimens...  21.7 us
    all_gather x1, blocking collectives, shards(): full_rows = lax.all_gather(row_sums, 'tp', axis=1, tiled=True)  11.9 us
    dynamic_slice x24, local copies, waits for them, and re-layouts, shards(): local_state, unused_steps = lax.scan(state_only, empty_state, block_inputs)  10.5 us
  transfers between devices with their start and end apart: 4, of which 3 were waited for; matrix products, arithmetic and copies ran while one was open for 4% of the time, Pallas kernels for 0%

commit v1 on v0

--- a/solution.py
+++ b/solution.py
@@ -9,6 +9,19 @@
 KCONV = 4
 BLOCK = 64
 HIGHEST_PRECISION = lax.Precision.HIGHEST
+
+
+def ring_gather(x, axis, dim):
+    ways = lax.axis_size(axis)
+    up = [(d, (d + 1) % ways) for d in range(ways)]
+    down = [(d, (d - 1) % ways) for d in range(ways)]
+    earlier, later = ([x], [x])
+    for _ in range(ways // 2):
+        earlier.append(lax.ppermute(earlier[-1], axis, up))
+    for _ in range((ways - 1) // 2):
+        later.append(lax.ppermute(later[-1], axis, down))
+    line = jnp.concatenate([*earlier[::-1], *later[1:]], axis=dim)
+    return jnp.roll(line, (lax.axis_index(axis) - ways // 2) * x.shape[dim], axis=dim)
 
 
 def prefix(array, axis, combine, identity):
@@ -277,7 +290,7 @@
         lax.psum(conv_edges.astype(jnp.bfloat16), "seq").astype(jnp.float32),
         lax.psum(end_states.astype(jnp.bfloat16), "seq").astype(jnp.float32),
     )
-    full_rows = lax.all_gather(row_sums, "tp", axis=1, tiled=True)
+    full_rows = ring_gather(row_sums, "tp", 1)
     mean_square = jnp.mean(full_rows * full_rows, axis=1)
     last_norms = jnp.sqrt(mean_square)
     final_rows = (full_rows * lax.rsqrt(mean_square[:, None] + 1e-06) * final_gain).astype(

time: 480 us -> 377 us (0.79)
  waiting for transfers between devices: 147 us -> 50.3 us
  blocking collectives: 165 us -> 154 us
    psum x1, waiting for transfers between devices: 96.7 us -> 0.02 us  [shards(): lax.psum(end_states.astype(jnp.bfloat16), 'seq').astype(jnp.float32)]
    all_gather x1 -> x0, blocking collectives: 11.9 us -> none  [shards(): full_rows = lax.all_gather(row_sums, 'tp', axis=1, tiled=True)]
    ppermute x0 -> x3, waiting for transfers between devices: none -> 5.72 us  [the longest x2 4.95 us: ring_gather(): earlier.append(lax.ppermute(earlier[-1], axis, up))]
    reduce_scatter x1, waiting for transfers between devices: 21.7 us -> 16.2 us  [shards(): lax.psum_scatter(projected_out.astype(jnp.bfloat16), 'tp', scatter_dimens...]
  transfers between devices with their start and end apart: 4 -> 7, of which waited for: 3 -> 4; matrix products, arithmetic and copies ran while one was open for 4% -> 5% of each run, Pallas kernels for 0% -> 0%
where the time goes in v1:
time: 377 us; the launch traced here: 374 us
  blocking collectives  154 us (41%)
  other arithmetic  82.7 us (22%)
  waiting for transfers between devices  50.3 us (13%)
  local copies, waits for them, and re-layouts  27.5 us (7%)
  matrix products  24.9 us (7%)
  between operations  15.4 us (4%)
  loops' own time  14.8 us (4%)
  starting transfers between devices  4.63 us (1%)
    psum x1, blocking collectives, shards(): lax.psum(conv_edges.astype(jnp.bfloat16), 'seq').astype(jnp.float32)  127 us
    select_n x32, other arithmetic, hop(): return jax.tree.map(lambda a, b: jnp.where(reached, a, b), new, before)  34.9 us
    all_gather x1, waiting for transfers between devices, prefix(): lax.all_gather(part.astype(kind), axis)  28.3 us
    all_gather x1, blocking collectives, prefix(): lax.all_gather(part.astype(kind), axis)  27 us
    reduce_scatter x1, waiting for transfers between devices, shards(): lax.psum_scatter(projected_out.astype(jnp.bfloat16), 'tp', scatter_dimens...  16.2 us
    dynamic_slice x24, local copies, waits for them, and re-layouts, shards(): local_state, unused_steps = lax.scan(state_only, empty_state, block_inputs)  10.5 us
    another operation x1, loops' own time, shards(): lax.scan(stepper, (incoming, empty_ends), block_inputs)  8.27 us
    reduce_sum x4, other arithmetic, block_step(): jnp.sum(query_rows[:, None] * key_floats[None, :] * weights, axis=-1)  8.17 us
  transfers between devices with their start and end apart: 7, of which 4 were waited for; matrix products, arithmetic and copies ran while one was open for 5% of the time, Pallas kernels for 0%

profile of v1, /device:TPU:0, one launch (start us, length us, event | category | flops | bytes accessed | tf_op | source)
XLA Modules:
  0.0 374.3 jit_solution(11135848003077636718)
XLA Ops:
  7.2 1.6 multiply_reduce_fusion.1
  9.0 3.9 %convolution_convert_fusion.1 = bf16[256,1024]{1,0:T(8,128)(2,1)S(1)} fusion(bf16[2048,1024]{1,0:T(8,128)(2,1)} %param.24, f32[2048]{0:T(1024)} %param.23, f32[256]{0:T(256)S(1)} %add_rsqrt_fusion.1, bf16[256,2048]{1,0:T(8,128)(2,1)} %param.22), kind=kOutput, calls=%fused_computation.94 | convolution fusion | flops 1076101120 | bytes 5776384 | tf_op jit(solution)/shard_map/dot_general | solution.py:227
  17.8 2.1 pad_maximum_fusion
  21.7 21.8 %while.43 = (s32[]{:T(128)}, f32[1,256,512]{2,1,0:T(8,128)S(1)}, s32[4,64]{1,0:T(4,128)S(1)}, s32[4]{0:T(128)S(1)}, f32[4,64,1,256]{3,2,1,0:T(1,128)}, /*index=5...) while((s32[]{:T(128)}, f32[1,256,512]{2,1,0:T(8,128)S(1)}, ...), condition=%wide.region_7.8_spmd.clone, body=%wide.region_5.7_spmd.clone.sunk | while | flops 18415684 | bytes 1417237 | solution.py:263
  46.2 27.0 %all-gather.2 = bf16[32,1,256]{2,1,0:T(2,128)(2,1)S(1)} all-gather(bf16[1,1,256]{2,1,0:T(2,128)(2,1)S(1)} %reshape.975), channel_id=2, replica_groups=mesh['seq'=32,'tp'=4] {'seq'}, dimensions={0}, use_global_device_ids=true | all-gather | bytes 16896 | tf_op jit(solution)/shard_map/all_gather | solution.py:30
  73.3 28.3 %all-gather.5.cloned.1.call-done = bf16[32,256,512]{2,1,0:T(8,128)(2,1)} async-done(((bf16[1,256,512]{2,1,0:T(8,128)(2,1)}), bf16[32,256,512]{2,1,0:T(8,128)(2,1)}) %all-gather.5.cloned.1.call-update) | async-done | bytes 8388624 | tf_op jit(solution)/shard_map/all_gather | solution.py:30
  101.6 36.2 %while.44 = (s32[]{:T(128)}, f32[1,256,512]{2,1,0:T(8,128)S(1)}, s32[]{:T(128)}, bf16[32,1,256]{2,1,0:T(2,128)(2,1)S(1)}, bf16[32,1,256,512]{3,2,1,0:T(8,128)(2,1)}, /*index=5*/s32[]{:T(128)}, s32[]{:T(128)}) while((s32[]{:T(128)}, f32[1,256,512]{2,1,0:T(8,128)S(1)}, s32[]{:T(128)}, bf16[32,1,256]{2,1,0:T(2,128)(2,1)S(1)}, ...), condition=%wide.region_9.10_spmd.clone, body=%wide.region_8.9_spmd.clone.sunk | while | flops 655620 | bytes 1313385 | solution.py:47
  139.3 54.6 %while.42 = (s32[]{:T(128)}, f32[1,256,512]{2,1,0:T(8,128)S(1)}, bf16[8,1,256,512]{3,2,0,1:T(8,128)(2,1)}, f32[4,64,1,512]{3,1,2,0:T(8,128)}, s32[4,64]{1,0:T(4,...) while((s32[]{:T(128)}, f32[1,256,512]{2,1,0:T(8,128)S(1)}, ...), condition=%wide.region_17.18_spmd, body=%wide.region_11.17_spmd.sunk | while | flops 268659424 | bytes 8804605 | solution.py:266
  145.0 5.8 %conditional.2 = (bf16[8,1,256,512]{3,2,0,1:T(8,128)(2,1)}) conditional(s32[]{:T(128)} %convert_element_type.390, bf16[8,1,256,512]{3,2,0,1:T(8,128)(2,1)} %get-tuple-element.722, (pred[8]{0:T(512)(128)(4,1)S(1)}, s32[8]{0:T(128)S(1)}, s32[64]{0:T(128)S(1)}, bf16[1,64,1,256]{3,2,1,0:T(2,128)(2,1)S(1)}, f32[64,1,256]{2,1,0:T(1,128)S(1)}, ...), branch_computations={%region_14.14_spmd, %region_15.15_spmd} | conditional | flops 139086368 | bytes 5199492 | solution.py:120
  147.0 3.7 fusion
  150.9 2.0 multiply_reduce_fusion.5
  163.2 2.0 multiply_reduce_fusion.5
  175.4 2.0 multiply_reduce_fusion.5
  187.6 2.0 multiply_reduce_fusion.5
  195.1 2.9 fusion.56
  198.0 1.7 convolution_convert_fusion
  201.5 1.7 gather_fusion.4
  203.2 1.7 gather_fusion.3
  204.9 1.7 gather_fusion.2
  206.9 16.2 %reduce-scatter.2.cloned.1.call-done = bf16[256,512]{1,0:T(8,128)(2,1)} async-done(((bf16[256,2048]{1,0:T(8,128)(2,1)}), bf16[256,512]{1,0:T(8,128)(2,1)}) %reduce-scatter.2.cloned.1.call-update) | async-done | bytes 262160 | tf_op jit(solution)/shard_map/reduce_scatter | solution.py:270
  224.9 127.2 %all-reduce = (bf16[8,3,1024]{2,0,1:T(8,128)(2,1)S(1)}, bf16[8,512]{1,0:T(8,128)(2,1)S(1)}) all-reduce(bf16[8,3,1024]{2,0,1:T(8,128)(2,1)S(1)} %pad_maximum_fusion.1, bf16[8,512]{1,0:T(8,128)(2,1)S(1)} %select_convert_fusion.2), channel_id=1, replica_groups=mesh['seq'=32,'tp'=4] {'seq'}, use_global_device_ids=true, to_apply=%region_21.22 | all-reduce | flops 28672 | bytes 114688 | tf_op jit(solution)/shard_map/psum | solution.py:290
  352.2 4.9 %collective-permute-done.1 = f32[8,512]{1,0:T(8,128)S(1)} collective-permute-done((f32[8,512]{1,0:T(8,128)S(1)}, f32[8,512]{1,0:T(8,128)S(1)}, u32[]{:S(2)}, u32[]{:S(2)}) %collective-permute-start.1) | collective-permute-done | bytes 16416 | tf_op jit(solution)/shard_map/ppermute | solution.py:20
  357.1 4.3 %convert_element_type.304 = f32[8,1,256,512]{3,2,1,0:T(8,128)} convert(bf16[8,1,256,512]{3,2,1,0:T(8,128)(2,1)} %all-reduce.3.cloned.1.call-done) | non-fusion elementwise | flops 1048576 | bytes 6291456 | tf_op jit(solution)/shard_map/convert_element_type | solution.py:291
  361.4 3.2 collective-permute-start.3
  (300 shorter events, 103.8 us)
Async XLA Ops:
  7.2 190.8 %copy-start = (bf16[512,2048]{1,0:T(8,128)(2,1)S(1)}, bf16[512,2048]{1,0:T(8,128)(2,1)}, u32[]{:S(2)}) copy-start(bf16[512,2048]{1,0:T(8,128)(2,1)} %param.31) | copy-start | bytes 6291460
  7.2 94.4 %all-gather.5.cloned.1.call-start = ((), (), s32[]{:S(2)}) async-start(), calls=%async_computation.3 | async-start | bytes 8650752 | tf_op jit(solution)/shard_map/all_gather | solution.py:30
  8.9 6.1 %copy-start.8 = (s32[8]{0:T(128)S(1)}, s32[8]{0:T(128)}, u32[]{:S(2)}) copy-start(s32[8]{0:T(128)} %param.34) | copy-start | bytes 100
  8.9 6.1 %copy-start.14 = (s32[8]{0:T(128)S(1)}, s32[8]{0:T(128)}, u32[]{:S(2)}) copy-start(s32[8]{0:T(128)} %param.35) | copy-start | bytes 100
  8.9 6.7 %copy-start.6 = (f32[4,1024]{1,0:T(4,128)S(1)}, f32[4,1024]{1,0:T(4,128)}, u32[]{:S(2)}) copy-start(f32[4,1024]{1,0:T(4,128)} %param.25) | copy-start | bytes 49156
  8.9 6.7 %copy-start.1 = (bf16[256,2048]{1,0:T(8,128)(2,1)S(1)}, bf16[256,2048]{1,0:T(8,128)(2,1)}, u32[]{:S(2)}) copy-start(bf16[256,2048]{1,0:T(8,128)(2,1)} %param.22) | copy-start | bytes 3145732
  8.9 6.7 %copy-start.9 = (bf16[2048,16]{0,1:T(8,128)(2,1)S(1)}, bf16[2048,16]{0,1:T(8,128)(2,1)}, u32[]{:S(2)}) copy-start(bf16[2048,16]{0,1:T(8,128)(2,1)} %param.26) | copy-start | bytes 196612
  8.9 6.7 %copy-start.11 = (f32[2048]{0:T(1024)S(1)}, f32[2048]{0:T(1024)}, u32[]{:S(2)}) copy-start(f32[2048]{0:T(1024)} %param.23) | copy-start | bytes 24580
  9.0 7.1 %copy-start.10 = (bf16[16,256]{1,0:T(8,128)(2,1)S(1)}, bf16[16,256]{1,0:T(8,128)(2,1)}, u32[]{:S(2)}) copy-start(bf16[16,256]{1,0:T(8,128)(2,1)} %param.27) | copy-start | bytes 24580
  9.0 7.1 %copy-start.13 = (f32[256]{0:T(256)S(1)}, f32[256]{0:T(256)}, u32[]{:S(2)}) copy-start(f32[256]{0:T(256)} %param.28) | copy-start | bytes 3076
  12.9 0.8 copy-start.4
  13.7 4.1 %collective-permute-start = (bf16[3,1024]{1,0:T(4,128)(2,1)S(1)}, bf16[3,1024]{1,0:T(4,128)(2,1)S(1)}, u32[]{:S(2)}, u32[]{:S(2)}) collective-permute-start(bf16[3,1024]{1,0:T(4,128)(2,1)S(1)} %slice.111), channel_id=1, source_target_pairs={{0,4},{4,8},{8,12},{12,16},{16,20},{20,24},{24,28},{28,32},{32,36}... | collective-permute-start | bytes 18440 | tf_op jit(solution)/shard_map/ppermute | solution.py:53
  44.3 178.8 %reduce-scatter.2.cloned.1.call-start = ((), (), s32[]{:S(2)}) async-start(), calls=%async_computation.1 | async-start | bytes 1310720 | tf_op jit(solution)/shard_map/reduce_scatter | solution.py:270
  139.3 55.9 %copy-start.12 = (f32[512]{0:T(512)S(1)}, f32[512]{0:T(512)}, u32[]{:S(2)}) copy-start(f32[512]{0:T(512)} %param.30) | copy-start | bytes 6148
  198.0 1.8 copy-start.2
  199.8 157.3 %all-reduce.3.cloned.1.call-start = ((), (), s32[]{:S(2)}) async-start(), calls=%async_computation.2 | async-start | bytes 4194304 | tf_op jit(solution)/shard_map/psum | solution.py:291
  224.3 137.1 %copy-start.5 = (bf16[256,512]{1,0:T(8,128)(2,1)}, bf16[256,512]{1,0:T(8,128)(2,1)S(1)}, u32[]{:S(2)}) copy-start(bf16[256,512]{1,0:T(8,128)(2,1)S(1)} %add_convert_fusion) | copy-start | bytes 786436
  352.2 4.9 %collective-permute-start.1 = (f32[8,512]{1,0:T(8,128)S(1)}, f32[8,512]{1,0:T(8,128)S(1)}, u32[]{:S(2)}, u32[]{:S(2)}) collective-permute-start(f32[8,512]{1,0:T(8,128)S(1)} %convert_element_type.314), channel_id=1, source_target_pairs={{0,1},{1,2},{2,3},{3,0},{4,5},{5,6},{6,7},{7,4},{8,9},{9,10},{10,1... | collective-permute-start | bytes 49160 | tf_op jit(solution)/shard_map/ppermute | solution.py:20
  357.1 8.2 %collective-permute-start.2 = (f32[8,512]{1,0:T(8,128)S(1)}, f32[8,512]{1,0:T(8,128)S(1)}, u32[]{:S(2)}, u32[]{:S(2)}) collective-permute-start(f32[8,512]{1,0:T(8,128)S(1)} %collective-permute-done.1), channel_id=1, source_target_pairs={{0,1},{1,2},{2,3},{3,0},{4,5},{5,6},{6,7},{7,4},{8,9},{9,10},{10,1... | collective-permute-start | bytes 49160 | tf_op jit(solution)/shard_map/ppermute | solution.py:20
  357.1 9.6 %copy-start.3 = (bf16[250,2048]{1,0:T(8,128)(2,1)S(1)}, bf16[250,2048]{1,0:T(8,128)(2,1)}, u32[]{:S(2)}) copy-start(bf16[250,2048]{1,0:T(8,128)(2,1)} %param.33) | copy-start | bytes 3072004
  357.1 9.6 %copy-start.7 = (f32[2048]{0:T(1024)S(1)}, f32[2048]{0:T(1024)}, u32[]{:S(2)}) copy-start(f32[2048]{0:T(1024)} %param.32) | copy-start | bytes 24580
  361.4 4.7 %collective-permute-start.3 = (f32[8,512]{1,0:T(8,128)S(1)}, f32[8,512]{1,0:T(8,128)S(1)}, u32[]{:S(2)}, u32[]{:S(2)}) collective-permute-start(f32[8,512]{1,0:T(8,128)S(1)} %convert_element_type.314), channel_id=1, source_target_pairs={{0,3},{1,0},{2,1},{3,2},{4,7},{5,4},{6,5},{7,6},{8,11},{9,8},{10,9... | collective-permute-start | bytes 49160 | tf_op jit(solution)/shard_map/ppermute | solution.py:22
Sparse Core Ops, SparseCore 0:
  44.4 57.1 all-gather.4
  199.9 23.1 reduce-scatter.1
  226.9 107.3 all-reduce.2
